TPU v7x, 256 devices: a whole 4x4x8 slice. The times are simulated.
256 devices in a mesh: tm: 16 (over z, x_hi), height: 4 (over x_lo, core), mp: 4 (over y).
Axes of the slice: x: 4 (x_hi: 2, x_lo: 2; x = x_hi * 2 + x_lo), y: 4, z: 8, core: 2. Of those that a mesh axis runs over, the one named last changes fastest.
Arguments:
- image_q: bfloat16 [16, 4, 384, 3072], P('tm', 'height', None, 'mp'), may hold values from -8 to 8
- image_kv: bfloat16 [16, 4, 2, 384, 3072], P('tm', 'height', None, None, 'mp'), may hold values from -8 to 8
- text_kv: bfloat16 [2, 256, 3072], P(None, 'tm', 'mp'), may hold values from -8 to 8
- residual: bfloat16 [16, 4, 384, 3072], P('tm', 'height', None, 'mp'), may hold values from -3 to 3
- out_weight: bfloat16 [3072, 3072], P('mp'), may hold values from -0.109375 to 0.109375
- out_gate: float32 [3072], P('mp'), may hold values from 0.5 to 2
- head_reach: int32 [24, 2], P('mp'), may hold values from 0 to 1, as said below
- tile_extent: int32 [2, 16, 4], replicated, may hold values from 1 to 8, as said below
Outputs:
- updated_tokens: bfloat16 [16, 4, 384, 3072], P('tm', 'height', None, 'mp')
Inputs may be any that keep to these rules, and one draw needn't show every extreme that they name: `head_reach`: in each column exactly 16 heads have reach 1, the others 0. `tile_extent`: valid frames are 6 except in the last tile row along time, where they are below 6; valid rows are 8 except in the last tile row along height, where they are below 8.
All inputs are finite; a program needn't handle non-finite values.
Results may differ from a plain program's by a relative error of at most 0.015.
Values may be sent and summed in bfloat16 or wider, within the bound.
No kernel may reach another device: no remote copies, remote signals or barrier semaphores. Data moves between devices by JAX's collectives and lax.ppermute only.
A program may use at most 128 MiB of HBM per device.

v0:
```python
import math
import jax
import jax.numpy as jnp
from jax import lax
from jax.sharding import PartitionSpec as P

HD = 128
TXT = 256
TILE_F = 6
TILE_R = 8
TILE_C = 8


def with_halo(array, sides, width):
    for axis, dim in sides:
        devices, length = (lax.axis_size(axis), array.shape[dim])
        up = [(i, (i + 1) % devices) for i in range(devices - 1)]
        down = [(j, i) for i, j in up]
        last = lax.slice_in_dim(array, length - width, length, axis=dim)
        leading = lax.slice_in_dim(array, 0, width, axis=dim)
        before = lax.ppermute(last, axis, up)
        after = lax.ppermute(leading, axis, down)
        array = jnp.concatenate([before, array, after], axis=dim)
    return array


def token_masks(extent_pair):
    positions = jnp.arange(TILE_F * TILE_R * TILE_C, dtype=jnp.int32)
    frame_of = positions // (TILE_R * TILE_C)
    row_of = positions // TILE_C % TILE_R
    frame_ok = frame_of < extent_pair[0][..., None]
    row_ok = row_of < extent_pair[1][..., None]
    return jnp.logical_and(frame_ok, row_ok)


def extend_tiles(image_kv):
    return with_halo(image_kv, (("tm", 0), ("height", 1)), 1)


def per_device(image_q, image_kv, text_kv, residual, out_weight, out_gate, head_reach, tile_extent):
    tiles_local = image_q.shape[0]
    tile_len = image_q.shape[2]
    col_width = image_q.shape[3]
    heads_here = col_width // HD
    text_both = lax.all_gather(text_kv, "tm", axis=1, tiled=True)
    extended = extend_tiles(image_kv)
    time_start = lax.axis_index("tm") * tiles_local
    height_start = lax.axis_index("height")
    zero_index = jnp.int32(0)
    padded_ext = jnp.pad(tile_extent, ((0, 0), (1, 1), (1, 1)))
    local_ext = lax.dynamic_slice(
        padded_ext, (zero_index, time_start, height_start), (2, tiles_local + 2, 3)
    )
    key_valid = token_masks(local_ext)
    flat_valid = key_valid[1:-1, 1]
    flat_q = image_q.reshape(tiles_local, tile_len, col_width)
    offsets = jnp.abs(jnp.arange(3, dtype=jnp.int32) - 1)
    scale_factor = 1.0 / math.sqrt(HD)

    def one_tile(tile_index):
        key_rows = jnp.concatenate([extended[:, :, 0].reshape(-1, col_width), text_both[0]], axis=0)
        value_rows = jnp.concatenate(
            [extended[:, :, 1].reshape(-1, col_width), text_both[1]], axis=0
        )
        queries = lax.dynamic_index_in_dim(flat_q, tile_index, 0, keepdims=False)

        def one_head(packed):
            head_id, reaches = packed
            column_start = head_id * HD
            q_head = lax.dynamic_slice_in_dim(queries, column_start, HD, 1)
            k_head = lax.dynamic_slice_in_dim(key_rows, column_start, HD, 1)
            v_head = lax.dynamic_slice_in_dim(value_rows, column_start, HD, 1)
            image_ok = jnp.logical_and(key_valid, offsets[:, None, None] <= reaches[0])
            image_ok = jnp.logical_and(image_ok, offsets[None, :, None] <= reaches[1])
            allowed = jnp.concatenate([image_ok.reshape(-1), jnp.ones((TXT,), jnp.bool_)])
            scores = (
                lax.dot_general(
                    q_head, k_head, (((1,), (1,)), ((), ())), preferred_element_type=jnp.float32
                )
                * scale_factor
            )
            masked = jnp.where(allowed[None, :], scores, -1e30)
            top_score = jnp.max(masked, axis=1, keepdims=True)
            weights = jnp.where(allowed[None, :], jnp.exp(masked - top_score), 0.0)
            row_total = jnp.sum(weights, axis=1, keepdims=True)
            return (
                jnp.dot(weights.astype(jnp.bfloat16), v_head, preferred_element_type=jnp.float32)
                / row_total
            )

        per_head = lax.map(one_head, (jnp.arange(heads_here, dtype=jnp.int32), head_reach))
        joined = jnp.transpose(per_head, (1, 0, 2)).reshape(tile_len, col_width)
        valid_rows = lax.dynamic_index_in_dim(flat_valid, tile_index, 0, keepdims=False)
        return jnp.where(valid_rows[:, None], joined, 0.0).astype(jnp.bfloat16)

    attended = lax.map(one_tile, jnp.arange(tiles_local, dtype=jnp.int32))
    projected = jnp.dot(
        attended.reshape(-1, col_width), out_weight, preferred_element_type=jnp.float32
    )
    summed = lax.psum_scatter(
        projected.reshape(tiles_local, 1, tile_len, -1).astype(jnp.bfloat16),
        "mp",
        scatter_dimension=3,
        tiled=True,
    ).astype(jnp.float32)
    return (residual.astype(jnp.float32) + out_gate * summed).astype(jnp.bfloat16)


def solution(mesh):
    return jax.shard_map(
        per_device,
        mesh=mesh,
        in_specs=(
            P("tm", "height", None, "mp"),
            P("tm", "height", None, None, "mp"),
            P(None, "tm", "mp"),
            P("tm", "height", None, "mp"),
            P("mp", None),
            P("mp"),
            P("mp", None),
            P(),
        ),
        out_specs=P("tm", "height", None, "mp"),
        check_vma=False,
    )
```

profile of v0, /device:TPU:1, one launch (start us, length us, event | category | flops | bytes accessed | tf_op | source)
XLA Modules:
  0.0 288.8 jit_solution(14104560325803142447)
XLA Ops:
  6.5 5.7 %collective-permute-start = (bf16[1,1,2,384,768]{4,3,2,1,0:T(8,128)(2,1)}, bf16[1,1,2,384,768]{4,3,2,1,0:T(8,128)(2,1)S(1)}, u32[]{:S(2)}, u32[]{:S(2)}) collective-permute-start(bf16[1,1,2,384,768]{4,3,2,1,0:T(8,128)(2,1)} %param.11), channel_id=1, source_target_pairs={{0,16},{16,32},{32,48},{48,64},{64,80},{80,96},{96,112},{112,128},... | collective-permute-start | bytes 3538952 | tf_op jit(solution)/shard_map/ppermute | solution.py:21
  12.2 1.3 collective-permute-start.1
  13.5 48.8 %collective-permute-done = bf16[1,1,2,384,768]{4,3,2,1,0:T(8,128)(2,1)S(1)} collective-permute-done((bf16[1,1,2,384,768]{4,3,2,1,0:T(8,128)(2,1)}, bf16[1,1,2,384,768]{4,3,2,1,0:T(8,128)(2,1)S(1)}, u32[]{:S(2)}, u32[]{:S(2)}) %collective-permute-start) | collective-permute-done | bytes 1179680 | tf_op jit(solution)/shard_map/ppermute | solution.py:21
  62.4 1.4 constant_dynamic-update-slice_fusion.2
  63.9 3.7 %collective-permute-start.2 = (bf16[3,1,2,384,768]{4,3,2,1,0:T(8,128)(2,1)S(1)}, bf16[3,1,2,384,768]{4,3,2,1,0:T(8,128)(2,1)}, u32[]{:S(2)}, u32[]{:S(2)}) collective-permute-start(bf16[3,1,2,384,768]{4,3,2,1,0:T(8,128)(2,1)S(1)} %constant_dynamic-update-slice_fusion.1), channel_id=1, source_target_pairs={{0,4},{4,8},{8,12},{1,5},{5,9},{9,13},{2,6},{6,10},{10,14},{3,7},{... | collective-permute-start | bytes 10616840 | tf_op jit(solution)/shard_map/ppermute | solution.py:21
  67.6 2.8 collective-permute-start.3
  70.7 0.6 slice.44
  71.3 0.6 slice.45
  71.9 1.7 and_reduce_fusion
  73.6 76.8 %all_gather.3 = bf16[2,256,768]{2,1,0:T(8,128)(2,1)S(1)} all-gather(bf16[2,16,768]{2,1,0:T(8,128)(2,1)} %param.12), channel_id=1, replica_groups=mesh['tm'=16,'height'=4,'mp'=4] {'tm'}, dimensions={1}, use_global_device_ids=true | all-gather | bytes 835584 | tf_op jit(solution)/shard_map/all_gather | solution.py:45
  150.4 1.0 slice_bitcast_fusion
  151.4 8.2 %pad_maximum_fusion = bf16[3,3,2,384,768]{4,3,2,1,0:T(8,128)(2,1)} fusion(bf16[3,1,2,384,768]{4,3,2,1,0:T(8,128)(2,1)} %collective-permute-done.3, bf16[3,1,2,384,768]{4,3,2,1,0:T(8,128)(2,1)S(1)} %constant_dynamic-update-slice_fusion.1, bf16[3,1,2,384,768]{4,3,2,1,0:T(8,128)(2,1)} %collective-permute-done.2), kind=kLoop, calls=%fused_computation.26 | loop fusion | flops 10616832 | bytes 21233664 | tf_op jit(solution)/shard_map/concatenate | solution.py:23
  159.6 9.0 %fusion.37 = (bf16[3,3,1,384,768]{4,3,2,1,0:T(8,128)(2,1)}, bf16[3,3,1,384,768]{4,3,2,1,0:T(8,128)(2,1)}) fusion(bf16[3,3,2,384,768]{4,3,2,1,0:T(8,128)(2,1)} %pad_maximum_fusion), kind=kLoop, calls=%fused_computation.60 | loop fusion | bytes 21233664 | tf_op jit(solution)/shard_map/while/body/eval_jaxpr/slice | solution.py:63
  168.6 9.5 %pad_maximum_fusion.1 = (bf16[3712,768]{1,0:T(8,128)(2,1)}, bf16[3712,768]{1,0:T(8,128)(2,1)}) fusion(bf16[256,768]{1,0:T(8,128)(2,1)S(1)} %copy-done.1, bf16[3456,768]{1,0:T(8,128)(2,1)} %bitcast.33, bf16[256,768]{1,0:T(8,128)(2,1)S(1)} %copy-done, bf16[3456,768]{1,0:T(8,128)(2,1)} %bitcast.32), kind=kLoop, calls=%fused_computation.27 | loop fusion | flops 22806528 | bytes 22806528 | tf_op jit(solution)/shard_map/while/body/eval_jaxpr/concatenate | solution.py:61
  178.1 54.3 %while.19 = (s32[]{:T(128)}, bf16[6,384,128]{1,2,0:T(8,128)(2,1)S(1)}, s32[6,2]{0,1:T(2,128)S(1)}, s32[6]{0:T(128)S(1)}, bf16[384,768]{1,0:T(8,128)(2,1)}, /*ind...) while((s32[]{:T(128)}, ...), condition=%wide.region_3.4_spmd.clone.clone, body=%wide.region_0.3_spmd.clone.clone.sunk | while | flops 742752384 | bytes 19636056 | solution.py:91
  178.7 1.2 fusion.51
  180.0 0.6 dynamic_slice.60
  181.3 2.4 fusion.53
  183.7 1.2 fusion.54
  184.8 2.2 fusion.55
  187.7 1.2 fusion.51
  189.1 0.6 dynamic_slice.60
  190.3 2.4 fusion.53
  192.7 1.2 fusion.54
  193.9 2.2 fusion.55
  196.8 1.2 fusion.51
  198.1 0.6 dynamic_slice.60
  199.4 2.4 fusion.53
  201.8 1.2 fusion.54
  202.9 2.2 fusion.55
  205.8 1.2 fusion.51
  207.2 0.6 dynamic_slice.60
  208.4 2.4 fusion.53
  210.8 1.2 fusion.54
  212.0 2.2 fusion.55
  214.9 1.2 fusion.51
  216.2 0.6 dynamic_slice.60
  217.5 2.4 fusion.53
  219.9 1.2 fusion.54
  221.0 2.2 fusion.55
  223.9 1.2 fusion.51
  225.3 0.6 dynamic_slice.60
  226.5 2.4 fusion.53
  228.9 1.2 fusion.54
  230.1 2.2 fusion.55
  232.6 5.9 %fusion.27 = bf16[1,1,384,3072]{3,2,1,0:T(8,128)(2,1)} fusion(bf16[384,768]{0,1:T(8,128)(2,1)S(1)} %fusion.28, bf16[768,3072]{1,0:T(8,128)(2,1)} %param.14), kind=kOutput, calls=%fused_computation.30 | convolution fusion | flops 1813118976 | bytes 7667712 | tf_op jit(solution)/shard_map/dot_general | solution.py:97
  238.5 41.4 %reduce-scatter.2.cloned.1.call-done = bf16[1,1,384,768]{3,2,1,0:T(8,128)(2,1)} async-done(((bf16[1,1,384,3072]{3,2,1,0:T(8,128)(2,1)}), bf16[1,1,384,768]{3,2,1,0:T(8,128)(2,1)}) %reduce-scatter.2.cloned.1.call-update) | async-done | bytes 589840 | tf_op jit(solution)/shard_map/reduce_scatter | solution.py:100
  279.9 2.1 add_convert_fusion
  (72 shorter events, 5.8 us)
Async XLA Ops:
  6.5 63.9 %copy-start.6 = (s32[2,16,4]{1,2,0:T(4,128)S(1)}, s32[2,16,4]{1,2,0:T(4,128)}, u32[]{:S(2)}) copy-start(s32[2,16,4]{1,2,0:T(4,128)} %param.17) | copy-start | bytes 1540
  6.5 273.4 %reduce-scatter.2.cloned.1.call-start = ((), (), s32[]{:S(2)}) async-start(), calls=%async_computation.1 | async-start | bytes 2949120 | tf_op jit(solution)/shard_map/reduce_scatter | solution.py:100
  6.5 55.8 %collective-permute-start = (bf16[1,1,2,384,768]{4,3,2,1,0:T(8,128)(2,1)}, bf16[1,1,2,384,768]{4,3,2,1,0:T(8,128)(2,1)S(1)}, u32[]{:S(2)}, u32[]{:S(2)}) collective-permute-start(bf16[1,1,2,384,768]{4,3,2,1,0:T(8,128)(2,1)} %param.11), channel_id=1, source_target_pairs={{0,16},{16,32},{32,48},{48,64},{64,80},{80,96},{96,112},{112,128},... | collective-permute-start | bytes 3538952 | tf_op jit(solution)/shard_map/ppermute | solution.py:21
  12.2 51.6 %collective-permute-start.1 = (bf16[1,1,2,384,768]{4,3,2,1,0:T(8,128)(2,1)}, bf16[1,1,2,384,768]{4,3,2,1,0:T(8,128)(2,1)S(1)}, u32[]{:S(2)}, u32[]{:S(2)}) collective-permute-start(bf16[1,1,2,384,768]{4,3,2,1,0:T(8,128)(2,1)} %param.11), channel_id=1, source_target_pairs={{16,0},{32,16},{48,32},{64,48},{80,64},{96,80},{112,96},{128,112},... | collective-permute-start | bytes 3538952 | tf_op jit(solution)/shard_map/ppermute | solution.py:22
  63.9 87.5 %collective-permute-start.2 = (bf16[3,1,2,384,768]{4,3,2,1,0:T(8,128)(2,1)S(1)}, bf16[3,1,2,384,768]{4,3,2,1,0:T(8,128)(2,1)}, u32[]{:S(2)}, u32[]{:S(2)}) collective-permute-start(bf16[3,1,2,384,768]{4,3,2,1,0:T(8,128)(2,1)S(1)} %constant_dynamic-update-slice_fusion.1), channel_id=1, source_target_pairs={{0,4},{4,8},{8,12},{1,5},{5,9},{9,13},{2,6},{6,10},{10,14},{3,7},{... | collective-permute-start | bytes 10616840 | tf_op jit(solution)/shard_map/ppermute | solution.py:21
  67.6 83.8 %collective-permute-start.3 = (bf16[3,1,2,384,768]{4,3,2,1,0:T(8,128)(2,1)S(1)}, bf16[3,1,2,384,768]{4,3,2,1,0:T(8,128)(2,1)}, u32[]{:S(2)}, u32[]{:S(2)}) collective-permute-start(bf16[3,1,2,384,768]{4,3,2,1,0:T(8,128)(2,1)S(1)} %constant_dynamic-update-slice_fusion.1), channel_id=1, source_target_pairs={{4,0},{8,4},{12,8},{5,1},{9,5},{13,9},{6,2},{10,6},{14,10},{7,3},{... | collective-permute-start | bytes 10616840 | tf_op jit(solution)/shard_map/ppermute | solution.py:22
  159.6 9.0 %copy-start = (bf16[256,768]{1,0:T(8,128)(2,1)S(1)}, bf16[256,768]{1,0:T(8,128)(2,1)}, u32[]{:S(2)}) copy-start(bf16[256,768]{1,0:T(8,128)(2,1)} %get-tuple-element.164) | copy-start | bytes 1179652
  159.6 9.0 %copy-start.1 = (bf16[256,768]{1,0:T(8,128)(2,1)S(1)}, bf16[256,768]{1,0:T(8,128)(2,1)}, u32[]{:S(2)}) copy-start(bf16[256,768]{1,0:T(8,128)(2,1)} %get-tuple-element.165) | copy-start | bytes 1179652
  168.6 9.5 %copy-start.3 = (bf16[6,384,128]{1,2,0:T(8,128)(2,1)S(1)}, bf16[6,384,128]{1,2,0:T(8,128)(2,1)}, u32[]{:S(2)}) copy-start(bf16[6,384,128]{1,2,0:T(8,128)(2,1)} %custom-call.1) | copy-start | bytes 1769476
  168.6 9.5 %copy-start.4 = (s32[6,2]{0,1:T(2,128)S(1)}, s32[6,2]{0,1:T(2,128)}, u32[]{:S(2)}) copy-start(s32[6,2]{0,1:T(2,128)} %param.16) | copy-start | bytes 148
  178.1 54.3 %copy-start.7 = (pred[384]{0:T(512)(128)(4,1)S(1)}, pred[384]{0:T(512)(128)(4,1)}, u32[]{:S(2)}) copy-start(pred[384]{0:T(512)(128)(4,1)} %and_reduce_fusion) | copy-start | bytes 1156
  232.6 47.3 %copy-start.2 = (bf16[1,1,384,768]{3,2,1,0:T(8,128)(2,1)S(1)}, bf16[1,1,384,768]{3,2,1,0:T(8,128)(2,1)}, u32[]{:S(2)}) copy-start(bf16[1,1,384,768]{3,2,1,0:T(8,128)(2,1)} %param.13) | copy-start | bytes 1769476
  232.6 47.3 %copy-start.5 = (f32[768]{0:T(1024)S(1)}, f32[768]{0:T(1024)}, u32[]{:S(2)}) copy-start(f32[768]{0:T(1024)} %param.15) | copy-start | bytes 9220
Sparse Core Ops, SparseCore 0:
  238.6 41.2 reduce-scatter.1
where the time goes:
time: 290 us; the launch traced here: 289 us
  waiting for transfers between devices  90.3 us (31%)
  blocking collectives  76.8 us (26%)
  other arithmetic  36.3 us (13%)
  matrix products  33.1 us (11%)
  local copies, waits for them, and re-layouts  21.1 us (7%)
  between operations  13.5 us (5%)
  starting transfers between devices  13.4 us (5%)
  loops' own time  4.28 us (1%)
    all_gather x1, blocking collectives, per_device(): text_both = lax.all_gather(text_kv, 'tm', axis=1, tiled=True)  76.8 us
    ppermute x2, waiting for transfers between devices, with_halo(): before = lax.ppermute(last, axis, up)  48.8 us
    reduce_scatter x1, waiting for transfers between devices, per_device(): lax.psum_scatter(projected.reshape(tiles_local, 1, tile_len, -1).astype(j...  41.4 us
    dot_general x6, matrix products, one_head(): lax.dot_general(q_head, k_head, (((1,), (1,)), ((), ())), preferred_eleme...  14.3 us
    dot_general x6, matrix products, one_head(): jnp.dot(weights.astype(jnp.bfloat16), v_head, preferred_element_type=jnp....  12.9 us
    concatenate x1, other arithmetic, one_tile(): jnp.concatenate([extended[:, :, 0].reshape(-1, col_width), text_both[0]],...  9.48 us
    ppermute x2, starting transfers between devices, with_halo(): before = lax.ppermute(last, axis, up)  9.33 us
    slice x1, local copies, waits for them, and re-layouts, one_tile(): extended[:, :, 1].reshape(-1, col_width)  8.97 us
  transfers between devices with their start and end apart: 5, of which 2 were waited for; matrix products, arithmetic and copies ran while one was open for 2% of the time, Pallas kernels for 0%

commit v1 on v0

--- a/solution.py
+++ b/solution.py
@@ -42,7 +42,9 @@
     tile_len = image_q.shape[2]
     col_width = image_q.shape[3]
     heads_here = col_width // HD
-    text_both = lax.all_gather(text_kv, "tm", axis=1, tiled=True)
+    text_both = jnp.concatenate(
+        lax.all_to_all(jnp.stack([text_kv] * lax.axis_size("tm")), "tm", 0, 0), axis=1
+    )
     extended = extend_tiles(image_kv)
     time_start = lax.axis_index("tm") * tiles_local
     height_start = lax.axis_index("height")

time: 290 us -> 259 us (0.89)
  blocking collectives: 76.8 us -> 0 us
  waiting for transfers between devices: 90.3 us -> 121 us
  starting transfers between devices: 13.4 us -> 25.1 us
    all_gather x1 -> x0, blocking collectives: 76.8 us -> none  [per_device(): text_both = lax.all_gather(text_kv, 'tm', axis=1, tiled=True)]
    all_to_all x0 -> x1, waiting for transfers between devices: none -> 32.7 us  [per_device(): lax.all_to_all(jnp.stack([text_kv] * lax.axis_size('tm')), 'tm', 0, 0)]
    all_to_all x0 -> x1, starting transfers between devices: none -> 11.7 us  [per_device(): lax.all_to_all(jnp.stack([text_kv] * lax.axis_size('tm')), 'tm', 0, 0)]
  transfers between devices with their start and end apart: 5 -> 6, of which waited for: 2 -> 3; matrix products, arithmetic and copies ran while one was open for 2% -> 3% of each run, Pallas kernels for 0% -> 0%
where the time goes in v1:
time: 259 us; the launch traced here: 258 us
  waiting for transfers between devices  121 us (47%)
  other arithmetic  36.8 us (14%)
  matrix products  33.1 us (13%)
  starting transfers between devices  25.1 us (10%)
  local copies, waits for them, and re-layouts  23.6 us (9%)
  between operations  13.6 us (5%)
  loops' own time  4.28 us (2%)
    ppermute x2, waiting for transfers between devices, with_halo(): before = lax.ppermute(last, axis, up)  48.8 us
    reduce_scatter x1, waiting for transfers between devices, per_device(): lax.psum_scatter(projected.reshape(tiles_local, 1, tile_len, -1).astype(j...  39.4 us
    all_to_all x1, waiting for transfers between devices, per_device(): lax.all_to_all(jnp.stack([text_kv] * lax.axis_size('tm')), 'tm', 0, 0)  32.7 us
    dot_general x6, matrix products, one_head(): lax.dot_general(q_head, k_head, (((1,), (1,)), ((), ())), preferred_eleme...  14.3 us
    dot_general x6, matrix products, one_head(): jnp.dot(weights.astype(jnp.bfloat16), v_head, preferred_element_type=jnp....  12.9 us
    all_to_all x1, starting transfers between devices, per_device(): lax.all_to_all(jnp.stack([text_kv] * lax.axis_size('tm')), 'tm', 0, 0)  11.7 us
    concatenate x1, other arithmetic, one_tile(): jnp.concatenate([extended[:, :, 0].reshape(-1, col_width), text_both[0]],...  9.49 us
    ppermute x2, starting transfers between devices, with_halo(): before = lax.ppermute(last, axis, up)  9.33 us
  transfers between devices with their start and end apart: 6, of which 3 were waited for; matrix products, arithmetic and copies ran while one was open for 3% of the time, Pallas kernels for 0%

profile of v1, /device:TPU:1, one launch (start us, length us, event | category | flops | bytes accessed | tf_op | source)
XLA Modules:
  0.0 257.5 jit_solution(14476114087548947664)
XLA Ops:
  6.5 5.7 %collective-permute-start = (bf16[1,1,2,384,768]{4,3,2,1,0:T(8,128)(2,1)}, bf16[1,1,2,384,768]{4,3,2,1,0:T(8,128)(2,1)S(1)}, u32[]{:S(2)}, u32[]{:S(2)}) collective-permute-start(bf16[1,1,2,384,768]{4,3,2,1,0:T(8,128)(2,1)} %param.11), channel_id=1, source_target_pairs={{0,16},{16,32},{32,48},{48,64},{64,80},{80,96},{96,112},{112,128},... | collective-permute-start | bytes 3538952 | tf_op jit(solution)/shard_map/ppermute | solution.py:21
  12.2 1.3 collective-permute-start.1
  13.5 48.8 %collective-permute-done = bf16[1,1,2,384,768]{4,3,2,1,0:T(8,128)(2,1)S(1)} collective-permute-done((bf16[1,1,2,384,768]{4,3,2,1,0:T(8,128)(2,1)}, bf16[1,1,2,384,768]{4,3,2,1,0:T(8,128)(2,1)S(1)}, u32[]{:S(2)}, u32[]{:S(2)}) %collective-permute-start) | collective-permute-done | bytes 1179680 | tf_op jit(solution)/shard_map/ppermute | solution.py:21
  62.4 1.4 constant_dynamic-update-slice_fusion.2
  63.9 3.7 %collective-permute-start.2 = (bf16[3,1,2,384,768]{4,3,2,1,0:T(8,128)(2,1)S(1)}, bf16[3,1,2,384,768]{4,3,2,1,0:T(8,128)(2,1)}, u32[]{:S(2)}, u32[]{:S(2)}) collective-permute-start(bf16[3,1,2,384,768]{4,3,2,1,0:T(8,128)(2,1)S(1)} %constant_dynamic-update-slice_fusion.1), channel_id=1, source_target_pairs={{0,4},{4,8},{8,12},{1,5},{5,9},{9,13},{2,6},{6,10},{10,14},{3,7},{... | collective-permute-start | bytes 10616840 | tf_op jit(solution)/shard_map/ppermute | solution.py:21
  67.5 2.8 %collective-permute-start.3 = (bf16[3,1,2,384,768]{4,3,2,1,0:T(8,128)(2,1)S(1)}, bf16[3,1,2,384,768]{4,3,2,1,0:T(8,128)(2,1)}, u32[]{:S(2)}, u32[]{:S(2)}) collective-permute-start(bf16[3,1,2,384,768]{4,3,2,1,0:T(8,128)(2,1)S(1)} %constant_dynamic-update-slice_fusion.1), channel_id=1, source_target_pairs={{4,0},{8,4},{12,8},{5,1},{9,5},{13,9},{6,2},{10,6},{14,10},{7,3},{... | collective-permute-start | bytes 10616840 | tf_op jit(solution)/shard_map/ppermute | solution.py:22
  70.4 1.0 stack.2
  71.4 11.7 %all-to-all-start = ((bf16[16,2,16,768]{3,2,1,0:T(8,128)(2,1)}), bf16[16,2,16,768]{3,2,1,0:T(8,128)(2,1)}, u32[]{:S(2)}, u32[]{:S(2)}) async-start(bf16[16,2,16,768]{3,2,1,0:T(8,128)(2,1)} %stack.2), calls=%async_computation | async-start | bytes 1572864 | tf_op jit(solution)/shard_map/all_to_all | solution.py:46
  83.4 0.6 slice.46
  84.1 0.6 slice.47
  84.7 1.8 and_reduce_fusion
  86.5 32.7 %all-to-all-done = bf16[16,2,16,768]{3,2,1,0:T(8,128)(2,1)} async-done(((bf16[16,2,16,768]{3,2,1,0:T(8,128)(2,1)}), bf16[16,2,16,768]{3,2,1,0:T(8,128)(2,1)}, u32[]{:S(2)}, u32[]{:S(2)}) %all-to-all-start) | async-done | bytes 786464 | tf_op jit(solution)/shard_map/all_to_all | solution.py:46
  119.1 2.1 fusion.38
  121.2 8.2 %pad_maximum_fusion = bf16[3,3,2,384,768]{4,3,2,1,0:T(8,128)(2,1)} fusion(bf16[3,1,2,384,768]{4,3,2,1,0:T(8,128)(2,1)} %collective-permute-done.3, bf16[3,1,2,384,768]{4,3,2,1,0:T(8,128)(2,1)S(1)} %constant_dynamic-update-slice_fusion.1, bf16[3,1,2,384,768]{4,3,2,1,0:T(8,128)(2,1)} %collective-permute-done.2), kind=kLoop, calls=%fused_computation.26 | loop fusion | flops 10616832 | bytes 21233664 | tf_op jit(solution)/shard_map/concatenate | solution.py:23
  129.4 9.0 %fusion.37 = (bf16[3,3,1,384,768]{4,3,2,1,0:T(8,128)(2,1)}, bf16[3,3,1,384,768]{4,3,2,1,0:T(8,128)(2,1)}) fusion(bf16[3,3,2,384,768]{4,3,2,1,0:T(8,128)(2,1)} %pad_maximum_fusion), kind=kLoop, calls=%fused_computation.58 | loop fusion | bytes 21233664 | tf_op jit(solution)/shard_map/while/body/eval_jaxpr/slice | solution.py:65
  138.4 9.5 %pad_maximum_fusion.1 = (bf16[3712,768]{1,0:T(8,128)(2,1)}, bf16[3712,768]{1,0:T(8,128)(2,1)}) fusion(bf16[256,768]{1,0:T(8,128)(2,1)S(1)} %bitcast.34, bf16[3456,768]{1,0:T(8,128)(2,1)} %bitcast.32, bf16[256,768]{1,0:T(8,128)(2,1)S(1)} %bitcast.33, bf16[3456,768]{1,0:T(8,128)(2,1)} %bitcast.31), kind=kLoop, calls=%fused_computation.27 | loop fusion | flops 22806528 | bytes 22806528 | tf_op jit(solution)/shard_map/while/body/eval_jaxpr/concatenate | solution.py:63
  148.0 55.1 %while.19 = (s32[]{:T(128)}, bf16[6,384,128]{1,2,0:T(8,128)(2,1)S(1)}, s32[6,2]{0,1:T(2,128)S(1)}, s32[6]{0:T(128)S(1)}, bf16[384,768]{1,0:T(8,128)(2,1)}, /*ind...) while((s32[]{:T(128)}, ...), condition=%wide.region_3.4_spmd.clone.clone, body=%wide.region_0.3_spmd.clone.clone.sunk | while | flops 742752384 | bytes 19636056 | solution.py:93
  148.6 1.3 fusion.52
  150.0 0.6 dynamic_slice.60
  151.3 2.4 fusion.54
  153.7 1.2 fusion.55
  154.8 2.2 fusion.56
  157.8 1.3 fusion.52
  159.2 0.6 dynamic_slice.60
  160.5 2.4 fusion.54
  162.9 1.2 fusion.55
  164.0 2.2 fusion.56
  167.0 1.3 fusion.52
  168.4 0.6 dynamic_slice.60
  169.6 2.4 fusion.54
  172.0 1.2 fusion.55
  173.2 2.2 fusion.56
  176.2 1.3 fusion.52
  178.8 2.4 fusion.54
  181.2 1.2 fusion.55
  182.4 2.2 fusion.56
  185.4 1.3 fusion.52
  186.8 0.6 dynamic_slice.60
  188.0 2.4 fusion.54
  190.4 1.2 fusion.55
  191.6 2.2 fusion.56
  194.6 1.3 fusion.52
  197.2 2.4 fusion.54
  199.6 1.2 fusion.55
  200.8 2.2 fusion.56
  203.3 5.9 %fusion.27 = bf16[1,1,384,3072]{3,2,1,0:T(8,128)(2,1)} fusion(bf16[384,768]{0,1:T(8,128)(2,1)S(1)} %fusion.28, bf16[768,3072]{1,0:T(8,128)(2,1)} %param.14), kind=kOutput, calls=%fused_computation.30 | convolution fusion | flops 1813118976 | bytes 7667712 | tf_op jit(solution)/shard_map/dot_general | solution.py:99
  209.2 39.4 %reduce-scatter.2.cloned.1.call-done = bf16[1,1,384,768]{3,2,1,0:T(8,128)(2,1)} async-done(((bf16[1,1,384,3072]{3,2,1,0:T(8,128)(2,1)}), bf16[1,1,384,768]{3,2,1,0:T(8,128)(2,1)}) %reduce-scatter.2.cloned.1.call-update) | async-done | bytes 589840 | tf_op jit(solution)/shard_map/reduce_scatter | solution.py:102
  248.6 2.1 add_convert_fusion
  (76 shorter events, 7.3 us)
Async XLA Ops:
  6.5 63.9 %copy-start.4 = (bf16[2,16,768]{2,1,0:T(8,128)(2,1)S(1)}, bf16[2,16,768]{2,1,0:T(8,128)(2,1)}, u32[]{:S(2)}) copy-start(bf16[2,16,768]{2,1,0:T(8,128)(2,1)} %param.12) | copy-start | bytes 147460
  6.5 76.6 %copy-start.7 = (s32[2,16,4]{1,2,0:T(4,128)S(1)}, s32[2,16,4]{1,2,0:T(4,128)}, u32[]{:S(2)}) copy-start(s32[2,16,4]{1,2,0:T(4,128)} %param.17) | copy-start | bytes 1540
  6.5 55.8 %collective-permute-start = (bf16[1,1,2,384,768]{4,3,2,1,0:T(8,128)(2,1)}, bf16[1,1,2,384,768]{4,3,2,1,0:T(8,128)(2,1)S(1)}, u32[]{:S(2)}, u32[]{:S(2)}) collective-permute-start(bf16[1,1,2,384,768]{4,3,2,1,0:T(8,128)(2,1)} %param.11), channel_id=1, source_target_pairs={{0,16},{16,32},{32,48},{48,64},{64,80},{80,96},{96,112},{112,128},... | collective-permute-start | bytes 3538952 | tf_op jit(solution)/shard_map/ppermute | solution.py:21
  12.2 51.6 %collective-permute-start.1 = (bf16[1,1,2,384,768]{4,3,2,1,0:T(8,128)(2,1)}, bf16[1,1,2,384,768]{4,3,2,1,0:T(8,128)(2,1)S(1)}, u32[]{:S(2)}, u32[]{:S(2)}) collective-permute-start(bf16[1,1,2,384,768]{4,3,2,1,0:T(8,128)(2,1)} %param.11), channel_id=1, source_target_pairs={{16,0},{32,16},{48,32},{64,48},{80,64},{96,80},{112,96},{128,112},... | collective-permute-start | bytes 3538952 | tf_op jit(solution)/shard_map/ppermute | solution.py:22
  63.9 57.4 %collective-permute-start.2 = (bf16[3,1,2,384,768]{4,3,2,1,0:T(8,128)(2,1)S(1)}, bf16[3,1,2,384,768]{4,3,2,1,0:T(8,128)(2,1)}, u32[]{:S(2)}, u32[]{:S(2)}) collective-permute-start(bf16[3,1,2,384,768]{4,3,2,1,0:T(8,128)(2,1)S(1)} %constant_dynamic-update-slice_fusion.1), channel_id=1, source_target_pairs={{0,4},{4,8},{8,12},{1,5},{5,9},{9,13},{2,6},{6,10},{10,14},{3,7},{... | collective-permute-start | bytes 10616840 | tf_op jit(solution)/shard_map/ppermute | solution.py:21
  67.5 53.7 %collective-permute-start.3 = (bf16[3,1,2,384,768]{4,3,2,1,0:T(8,128)(2,1)S(1)}, bf16[3,1,2,384,768]{4,3,2,1,0:T(8,128)(2,1)}, u32[]{:S(2)}, u32[]{:S(2)}) collective-permute-start(bf16[3,1,2,384,768]{4,3,2,1,0:T(8,128)(2,1)S(1)} %constant_dynamic-update-slice_fusion.1), channel_id=1, source_target_pairs={{4,0},{8,4},{12,8},{5,1},{9,5},{13,9},{6,2},{10,6},{14,10},{7,3},{... | collective-permute-start | bytes 10616840 | tf_op jit(solution)/shard_map/ppermute | solution.py:22
  71.4 47.7 %all-to-all-start = ((bf16[16,2,16,768]{3,2,1,0:T(8,128)(2,1)}), bf16[16,2,16,768]{3,2,1,0:T(8,128)(2,1)}, u32[]{:S(2)}, u32[]{:S(2)}) async-start(bf16[16,2,16,768]{3,2,1,0:T(8,128)(2,1)} %stack.2), calls=%async_computation | async-start | bytes 1572864 | tf_op jit(solution)/shard_map/all_to_all | solution.py:46
  83.1 165.6 %reduce-scatter.2.cloned.1.call-start = ((), (), s32[]{:S(2)}) async-start(), calls=%async_computation.2 | async-start | bytes 2949120 | tf_op jit(solution)/shard_map/reduce_scatter | solution.py:102
  129.4 9.0 %copy-start = (bf16[1,16,16,768]{3,2,0,1:T(8,128)(2,1)S(1)}, bf16[1,16,16,768]{3,2,0,1:T(8,128)(2,1)}, u32[]{:S(2)}) copy-start(bf16[1,16,16,768]{3,2,0,1:T(8,128)(2,1)} %get-tuple-element.164) | copy-start | bytes 1179652
  129.4 9.0 %copy-start.1 = (bf16[1,16,16,768]{3,2,0,1:T(8,128)(2,1)S(1)}, bf16[1,16,16,768]{3,2,0,1:T(8,128)(2,1)}, u32[]{:S(2)}) copy-start(bf16[1,16,16,768]{3,2,0,1:T(8,128)(2,1)} %get-tuple-element.165) | copy-start | bytes 1179652
  138.4 9.5 %copy-start.3 = (bf16[6,384,128]{1,2,0:T(8,128)(2,1)S(1)}, bf16[6,384,128]{1,2,0:T(8,128)(2,1)}, u32[]{:S(2)}) copy-start(bf16[6,384,128]{1,2,0:T(8,128)(2,1)} %custom-call.1) | copy-start | bytes 1769476
  138.4 9.5 %copy-start.5 = (s32[6,2]{0,1:T(2,128)S(1)}, s32[6,2]{0,1:T(2,128)}, u32[]{:S(2)}) copy-start(s32[6,2]{0,1:T(2,128)} %param.16) | copy-start | bytes 148
  148.0 55.1 %copy-start.8 = (pred[384]{0:T(512)(128)(4,1)S(1)}, pred[384]{0:T(512)(128)(4,1)}, u32[]{:S(2)}) copy-start(pred[384]{0:T(512)(128)(4,1)} %and_reduce_fusion) | copy-start | bytes 1156
  203.3 45.4 %copy-start.2 = (bf16[1,1,384,768]{3,2,1,0:T(8,128)(2,1)S(1)}, bf16[1,1,384,768]{3,2,1,0:T(8,128)(2,1)}, u32[]{:S(2)}) copy-start(bf16[1,1,384,768]{3,2,1,0:T(8,128)(2,1)} %param.13) | copy-start | bytes 1769476
  203.3 45.3 %copy-start.6 = (f32[768]{0:T(1024)S(1)}, f32[768]{0:T(1024)}, u32[]{:S(2)}) copy-start(f32[768]{0:T(1024)} %param.15) | copy-start | bytes 9220
Sparse Core Ops, SparseCore 0:
  209.3 39.2 reduce-scatter.1
